TPU v7x, 32 devices: a whole 2x2x4 slice. The times are simulated.
32 devices in a mesh: seq: 16 (over z, x, core), batch: 2 (over y).
Axes of the slice: x: 2, y: 2, z: 4, core: 2. Of those that a mesh axis runs over, the one named last changes fastest.
Arguments:
- activations: bfloat16 [2, 8192, 1536], P('batch', 'seq'), may hold values from -60 to 60
- cotangent: bfloat16 [2, 8192, 1536], P('batch', 'seq'), may hold values from -6 to 6
- contig_lengths: int32 [2, 4], P('batch'), may hold values from 1 to 4096, 8192 in all within a row
- gain_input: float32 [1536], replicated, may hold values from 0.1 to 1.9
- tap_weights: bfloat16 [3, 1536, 768], replicated, may hold values from -0.09375 to 0.09375
- gain_middle: float32 [768], replicated, may hold values from 0.1 to 1.9
- point_weights: bfloat16 [768, 1536], replicated, may hold values from -0.21875 to 0.21875
Outputs:
- block_output: bfloat16 [2, 8192, 1536], P('batch', 'seq')
- input_grad: bfloat16 [2, 8192, 1536], P('batch', 'seq')
- gain_input_grad: float32 [1536], replicated
- gain_middle_grad: float32 [768], replicated
Inputs may be any that keep to these rules, and one draw needn't show every extreme that they name: `contig_lengths`: row w lists in order the lengths of the 4 contigs packed into window w; they sum to 8192.
All inputs are finite; a program needn't handle non-finite values.
Results may differ from a plain program's by a relative error of at most 0.0065.
Values may be sent and summed in bfloat16 or wider, within the bound.
No kernel may reach another device: no remote copies, remote signals or barrier semaphores. Data moves between devices by JAX's collectives and lax.ppermute only.
A program may use at most 64 MiB of HBM per device.

v0:
```python
import math
import jax
import jax.numpy as jnp
from jax import lax
from jax.sharding import PartitionSpec as P

SPAN = 2
epsilon = 1e-06


def shifted(x, axis, by):
    peers = lax.axis_size(axis)
    pairs = [(i, i + by) for i in range(peers) if 0 <= i + by < peers]
    return lax.ppermute(x, axis, pairs)


def norm_activate(values, scales):
    mean_square = jnp.mean(values * values, axis=-1, keepdims=True)
    return jax.nn.gelu(values * lax.rsqrt(mean_square + epsilon) * scales, approximate=True)


def contig_owner(lengths, positions):
    bounds = jnp.cumsum(lengths)
    return jnp.sum((positions[:, None] >= bounds[None, :]).astype(jnp.int32), axis=1)


def body(
    activations, cotangent, contig_lengths, gain_input, tap_weights, gain_middle, point_weights
):
    signal = activations[0]
    upstream = cotangent[0]
    lengths = contig_lengths[0]
    shard_rows = signal.shape[0]
    seq_count = lax.axis_size("seq")
    tap_reach = SPAN * shard_rows
    total_length = shard_rows * seq_count
    positions = lax.axis_index("seq") * shard_rows + jnp.arange(shard_rows, dtype=jnp.int32)
    owners = contig_owner(lengths, positions)
    before_valid = (
        (positions >= tap_reach) & (contig_owner(lengths, positions - tap_reach) == owners)
    ).astype(jnp.float32)[:, None]
    after_valid = (
        (positions < total_length - tap_reach)
        & (contig_owner(lengths, positions + tap_reach) == owners)
    ).astype(jnp.float32)[:, None]
    tap_before = tap_weights[0]
    tap_center = tap_weights[1]
    tap_after = tap_weights[2]
    normed, input_vjp = jax.vjp(norm_activate, signal.astype(jnp.float32), gain_input)
    hidden = normed.astype(jnp.bfloat16)
    hidden_before = shifted(hidden, "seq", SPAN)
    hidden_after = shifted(hidden, "seq", -SPAN)
    combined = jnp.dot(hidden, tap_center, preferred_element_type=jnp.float32)
    combined = combined + before_valid * jnp.dot(
        hidden_before, tap_before, preferred_element_type=jnp.float32
    )
    combined = combined + after_valid * jnp.dot(
        hidden_after, tap_after, preferred_element_type=jnp.float32
    )
    middle_f, middle_vjp = jax.vjp(norm_activate, combined, gain_middle)
    middle = middle_f.astype(jnp.bfloat16)
    output = (
        signal.astype(jnp.float32)
        + jnp.dot(middle, point_weights, preferred_element_type=jnp.float32)
    ).astype(jnp.bfloat16)
    grad_middle = jnp.dot(upstream, point_weights.T, preferred_element_type=jnp.float32)
    grad_combined_f, middle_terms = middle_vjp(grad_middle)
    grad_combined = grad_combined_f.astype(jnp.bfloat16)
    grad_hidden = jnp.dot(grad_combined, tap_center.T, preferred_element_type=jnp.float32)
    forward_terms = jnp.dot(grad_combined, tap_after.T, preferred_element_type=jnp.float32)
    backward_terms = jnp.dot(grad_combined, tap_before.T, preferred_element_type=jnp.float32)
    terms_before = shifted(forward_terms.astype(jnp.bfloat16), "seq", SPAN).astype(
        forward_terms.dtype
    )
    terms_after = shifted(backward_terms.astype(jnp.bfloat16), "seq", -SPAN).astype(
        backward_terms.dtype
    )
    grad_hidden = grad_hidden + before_valid * terms_before + after_valid * terms_after
    grad_signal, input_terms = input_vjp(grad_hidden)
    grad_output = (upstream.astype(jnp.float32) + grad_signal).astype(jnp.bfloat16)
    summed = lax.psum((input_terms, middle_terms), ("seq", "batch"))
    factor = 1.0 / math.sqrt(lax.axis_size("batch") * seq_count * shard_rows)
    return (output[None], grad_output[None], summed[0] * factor, summed[1] * factor)


def solution(mesh):
    placed = (
        P("batch", "seq", None),
        P("batch", "seq", None),
        P("batch", None),
        P(),
        P(),
        P(),
        P(),
    )
    return jax.shard_map(
        body,
        mesh=mesh,
        in_specs=placed,
        out_specs=(P("batch", "seq", None), P("batch", "seq", None), P(), P()),
        check_vma=False,
    )
```

profile of v0, /device:TPU:0, one launch (start us, length us, event | category | flops | bytes accessed | tf_op | source)
XLA Modules:
  0.0 216.5 jit_solution(4614288820705404492)
XLA Ops:
  0.6 0.0 copy-start
  0.6 0.0 copy-start.1
  0.7 0.0 copy-start.4
  0.7 0.0 copy-start.6
  0.7 1.9 fusion.16
  2.6 0.1 copy-done.1
  2.7 3.2 %fusion.12 = bf16[512,1536]{1,0:T(8,128)(2,1)} fusion(bf16[1,512,1536]{2,1,0:T(8,128)(2,1)S(1)} %copy-done.1, f32[1536]{0:T(1024)} %param.10, f32[512]{0:T(512)S(1)} %fusion.88), kind=kLoop, calls=%fused_computation.18 | loop fusion | flops 9437184 | bytes 3153920 | tf_op jit(solution)/shard_map/convert_element_type | solution.py:50
  5.9 6.0 %collective-permute-start = (bf16[512,1536]{1,0:T(8,128)(2,1)}, bf16[512,1536]{1,0:T(8,128)(2,1)}, u32[]{:S(2)}, u32[]{:S(2)}) collective-permute-start(bf16[512,1536]{1,0:T(8,128)(2,1)} %fusion.12), channel_id=1, source_target_pairs={{0,4},{2,6},{4,8},{6,10},{8,12},{10,14},{12,16},{14,18},{16,20},{1... | collective-permute-start | bytes 4718600 | tf_op jit(solution)/shard_map/ppermute | solution.py:14
  11.9 1.3 collective-permute-start.1
  13.2 0.0 copy-done.6
  13.2 0.2 reduce-window.8
  13.4 0.1 convert_reduce_fusion.2
  13.5 0.0 copy-done.4
  13.5 4.4 %fusion.42 = f32[512,768]{1,0:T(8,128)S(1)} fusion(bf16[3,1536,768]{2,1,0:T(8,128)(2,1)} %param.11, bf16[1,512,1536]{2,1,0:T(8,128)(2,1)} %param.7, f32[1536]{0:T(1024)S(1)} %copy-done.4, f32[512]{0:T(512)S(1)} %fusion.88), kind=kOutput, calls=%fused_computation.51 | convolution fusion | flops 1217396736 | bytes 5513216 | tf_op jit(solution)/shard_map/dot_general | solution.py:53
  17.9 60.5 %collective-permute-done = bf16[512,1536]{1,0:T(8,128)(2,1)} collective-permute-done((bf16[512,1536]{1,0:T(8,128)(2,1)}, bf16[512,1536]{1,0:T(8,128)(2,1)}, u32[]{:S(2)}, u32[]{:S(2)}) %collective-permute-start) | collective-permute-done | bytes 1572896 | tf_op jit(solution)/shard_map/ppermute | solution.py:14
  78.4 3.5 %fusion.38 = f32[512,768]{1,0:T(8,128)S(1)} fusion(bf16[512,1536]{1,0:T(8,128)(2,1)} %collective-permute-done, bf16[3,1536,768]{2,1,0:T(8,128)(2,1)} %param.11), kind=kOutput, calls=%fused_computation.47 | convolution fusion | flops 1207959552 | bytes 5505024 | tf_op jit(solution)/shard_map/dot_general | solution.py:54
  81.9 0.0 collective-permute-done.1
  81.9 0.0 copy-start.3
  82.0 0.0 copy-start.5
  82.0 3.8 %multiply_reduce_fusion.2 = (f32[512]{0:T(512)S(1)}, f32[512,768]{1,0:T(8,128)S(1)}) fusion(bf16[512,1536]{1,0:T(8,128)(2,1)} %collective-permute-done.1, bf16[3,1536,768]{2,1,0:T(8,128)(2,1)} %param.11, f32[512]{0:T(512)S(1)} %get-tuple-element.14, f32[512,768]{1,0:T(8,128)S(1)} %fusion.42, f32[512,768]{1,0:T(8,128)S(1)} %fusion.38, ...), kind=kOutput, calls=%fused_computation.75 | convolution fusion | flops 1210318336 | bytes 8656896 | tf_op jit(solution)/shard_map/dot_general | solution.py:57
  85.8 0.0 slice-start
  85.8 0.0 copy-done
  85.8 0.0 copy-done.3
  85.8 0.0 copy-done.5
  85.9 0.0 slice-start.1
  85.9 2.5 %multiply_reduce_fusion = (f32[768]{0:T(1024)S(1)}, f32[512]{0:T(512)S(1)}, f32[512,768]{1,0:T(8,128)S(1)}) fusion(f32[512,768]{1,0:T(8,128)S(1)} %get-tuple-element.16, f32[512]{0:T(512)S(1)} %fusion.89, f32[768]{0:T(1024)S(1)} %copy-done.5, bf16[768,1536]{1,0:T(8,128)(2,1)S(1)} %copy-done, bf16[1,512,1536]{2,1,0:T(8,128)(2,1)S(1)} %copy-done.3), kind=kOutput, calls=%fused_computation.72 | convolution fusion | flops 1218181888 | bytes 7088128 | tf_op jit(solution)/shard_map/dot_general | solution.py:66
  88.4 0.4 fusion.58
  88.8 0.0 slice-done
  88.8 0.1 slice-done.1
  88.9 1.4 convolution_convert_fusion
  90.3 0.0 copy-start.2
  90.4 1.4 convolution_convert_fusion.1
  91.8 4.5 %collective-permute-start.2 = (bf16[512,1536]{1,0:T(8,128)(2,1)S(1)}, bf16[512,1536]{1,0:T(8,128)(2,1)S(1)}, u32[]{:S(2)}, u32[]{:S(2)}) collective-permute-start(bf16[512,1536]{1,0:T(8,128)(2,1)S(1)} %convolution_convert_fusion.1), channel_id=1, source_target_pairs={{0,4},{2,6},{4,8},{6,10},{8,12},{10,14},{12,16},{14,18},{16,20},{1... | collective-permute-start | bytes 4718600 | tf_op jit(solution)/shard_map/ppermute | solution.py:14
  96.3 1.5 collective-permute-start.3
  97.8 0.0 copy-done.2
  97.8 2.8 %fusion.33 = bf16[1,512,1536]{2,1,0:T(8,128)(2,1)} fusion(bf16[768,1536]{1,0:T(8,128)(2,1)S(1)} %copy-done, bf16[1,512,1536]{2,1,0:T(8,128)(2,1)S(1)} %copy-done.2, f32[512,768]{1,0:T(8,128)S(1)} %get-tuple-element.16, f32[768]{0:T(1024)S(1)} %copy-done.5, f32[512]{0:T(512)S(1)} %fusion.89), kind=kOutput, calls=%fused_computation.41 | convolution fusion | flops 1214644224 | bytes 7083008 | tf_op jit(solution)/shard_map/dot_general | solution.py:64
  100.6 62.0 %collective-permute-done.2 = bf16[512,1536]{1,0:T(8,128)(2,1)S(1)} collective-permute-done((bf16[512,1536]{1,0:T(8,128)(2,1)S(1)}, bf16[512,1536]{1,0:T(8,128)(2,1)S(1)}, u32[]{:S(2)}, u32[]{:S(2)}) %collective-permute-start.2) | collective-permute-done | bytes 1572896 | tf_op jit(solution)/shard_map/ppermute | solution.py:14
  162.6 0.0 collective-permute-done.3
  162.7 6.1 %fusion.15 = (f32[1536]{0:T(1024)S(1)}, f32[512]{0:T(512)S(1)}, f32[512,1536]{1,0:T(8,128)}) fusion(bf16[1,512,1536]{2,1,0:T(8,128)(2,1)S(1)} %copy-done.2, f32[512]{0:T(512)S(1)} %fusion.88, f32[1536]{0:T(1024)S(1)} %copy-done.4, bf16[512,1536]{1,0:T(8,128)(2,1)S(1)} %collective-permute-done.3, f32[512]{0:T(512)S(1)} %get-tuple-element.14, ...), kind=kOutput, calls=%fused_computation.21 | convolution fusion | flops 1233909760 | bytes 11032576 | tf_op jit(solution)/shard_map/dot_general | solution.py:69
  168.8 41.6 %all-reduce = (f32[1536]{0:T(1024)S(1)}, f32[768]{0:T(1024)S(1)}) all-reduce(f32[1536]{0:T(1024)S(1)} %get-tuple-element.4, f32[768]{0:T(1024)S(1)} %get-tuple-element.6), channel_id=1, replica_groups=mesh['seq'=16,'batch'=2] {'seq','batch'}, use_global_device_ids=true, to_apply=%region_9.10 | all-reduce | flops 2304 | bytes 18432 | tf_op jit(solution)/shard_map/psum | solution.py:81
  210.4 0.6 broadcast_multiply_fusion
  211.0 0.6 broadcast_multiply_fusion.1
  211.6 4.9 %fusion.59 = bf16[1,512,1536]{2,1,0:T(8,128)(2,1)} fusion(bf16[1,512,1536]{2,1,0:T(8,128)(2,1)} %param.7, f32[512,1536]{1,0:T(8,128)} %get-tuple-element.18, bf16[1,512,1536]{2,1,0:T(8,128)(2,1)} %param.8, f32[512]{0:T(512)S(1)} %multiply_multiply_fusion.6, f32[1536]{0:T(1024)S(1)} %copy-done.4, f32[512]{0:T(512)S(1)} %fusion.88), kind=kLoop, calls=%fused_computation.68 | loop fusion | flops 7077888 | bytes 7874560 | tf_op jit(solution)/shard_map/broadcast_in_dim | solution.py:83
  (8 shorter events, 0.1 us)
Async XLA Ops:
  0.6 85.2 %copy-start = (bf16[768,1536]{1,0:T(8,128)(2,1)S(1)}, bf16[768,1536]{1,0:T(8,128)(2,1)}, u32[]{:S(2)}) copy-start(bf16[768,1536]{1,0:T(8,128)(2,1)} %param.13) | copy-start | bytes 7077892
  0.6 2.0 copy-start.1
  0.7 12.8 %copy-start.4 = (f32[1536]{0:T(1024)S(1)}, f32[1536]{0:T(1024)}, u32[]{:S(2)}) copy-start(f32[1536]{0:T(1024)} %param.10) | copy-start | bytes 18436
  0.7 12.5 %copy-start.6 = (s32[1,4]{1,0:T(1,128)S(1)}, s32[1,4]{1,0:T(1,128)}, u32[]{:S(2)}) copy-start(s32[1,4]{1,0:T(1,128)} %param.9) | copy-start | bytes 52
  5.9 72.5 %collective-permute-start = (bf16[512,1536]{1,0:T(8,128)(2,1)}, bf16[512,1536]{1,0:T(8,128)(2,1)}, u32[]{:S(2)}, u32[]{:S(2)}) collective-permute-start(bf16[512,1536]{1,0:T(8,128)(2,1)} %fusion.12), channel_id=1, source_target_pairs={{0,4},{2,6},{4,8},{6,10},{8,12},{10,14},{12,16},{14,18},{16,20},{1... | collective-permute-start | bytes 4718600 | tf_op jit(solution)/shard_map/ppermute | solution.py:14
  11.9 70.0 %collective-permute-start.1 = (bf16[512,1536]{1,0:T(8,128)(2,1)}, bf16[512,1536]{1,0:T(8,128)(2,1)}, u32[]{:S(2)}, u32[]{:S(2)}) collective-permute-start(bf16[512,1536]{1,0:T(8,128)(2,1)} %fusion.12), channel_id=1, source_target_pairs={{4,0},{6,2},{8,4},{10,6},{12,8},{14,10},{16,12},{18,14},{20,16},{2... | collective-permute-start | bytes 4718600 | tf_op jit(solution)/shard_map/ppermute | solution.py:14
  81.9 3.9 %copy-start.3 = (bf16[1,512,1536]{2,1,0:T(8,128)(2,1)S(1)}, bf16[1,512,1536]{2,1,0:T(8,128)(2,1)}, u32[]{:S(2)}) copy-start(bf16[1,512,1536]{2,1,0:T(8,128)(2,1)} %param.8) | copy-start | bytes 4718596
  82.0 3.9 %copy-start.5 = (f32[768]{0:T(1024)S(1)}, f32[768]{0:T(1024)}, u32[]{:S(2)}) copy-start(f32[768]{0:T(1024)} %param.12) | copy-start | bytes 9220
  85.8 3.0 %slice-start = ((s8[7077888]{0:T(1024)(128)(4,1)}), s8[4194304]{0:T(1024)(128)(4,1)S(1)}, s32[]{:S(2)}) async-start(s8[7077888]{0:T(1024)(128)(4,1)} %bitcast.116), calls=%async_computation | async-start | bytes 8388608
  85.9 3.1 %slice-start.1 = ((s8[7077888]{0:T(1024)(128)(4,1)}), s8[2883584]{0:T(1024)(128)(4,1)S(1)}, s32[]{:S(2)}) async-start(s8[7077888]{0:T(1024)(128)(4,1)} %bitcast.116), calls=%async_computation.1 | async-start | bytes 5767168
  90.3 7.4 %copy-start.2 = (bf16[1,512,1536]{2,1,0:T(8,128)(2,1)S(1)}, bf16[1,512,1536]{2,1,0:T(8,128)(2,1)}, u32[]{:S(2)}) copy-start(bf16[1,512,1536]{2,1,0:T(8,128)(2,1)} %param.7) | copy-start | bytes 4718596
  91.8 70.9 %collective-permute-start.2 = (bf16[512,1536]{1,0:T(8,128)(2,1)S(1)}, bf16[512,1536]{1,0:T(8,128)(2,1)S(1)}, u32[]{:S(2)}, u32[]{:S(2)}) collective-permute-start(bf16[512,1536]{1,0:T(8,128)(2,1)S(1)} %convolution_convert_fusion.1), channel_id=1, source_target_pairs={{0,4},{2,6},{4,8},{6,10},{8,12},{10,14},{12,16},{14,18},{16,20},{1... | collective-permute-start | bytes 4718600 | tf_op jit(solution)/shard_map/ppermute | solution.py:14
  96.3 66.4 %collective-permute-start.3 = (bf16[512,1536]{1,0:T(8,128)(2,1)S(1)}, bf16[512,1536]{1,0:T(8,128)(2,1)S(1)}, u32[]{:S(2)}, u32[]{:S(2)}) collective-permute-start(bf16[512,1536]{1,0:T(8,128)(2,1)S(1)} %convolution_convert_fusion), channel_id=1, source_target_pairs={{4,0},{6,2},{8,4},{10,6},{12,8},{14,10},{16,12},{18,14},{20,16},{2... | collective-permute-start | bytes 4718600 | tf_op jit(solution)/shard_map/ppermute | solution.py:14
where the time goes:
time: 217 us
  waiting for transfers between devices  123 us (57%)
  blocking collectives  41.6 us (19%)
  matrix products  26.1 us (12%)
  starting transfers between devices  13.2 us (6%)
  other arithmetic  11.9 us (5%)
    ppermute x4, waiting for transfers between devices, shifted(): return lax.ppermute(x, axis, pairs)  123 us
    psum x1, blocking collectives, body(): summed = lax.psum((input_terms, middle_terms), ('seq', 'batch'))  41.6 us
    ppermute x4, starting transfers between devices, shifted(): return lax.ppermute(x, axis, pairs)  13.2 us
    dot_general x1, matrix products, body(): jnp.dot(grad_combined, tap_center.T, preferred_element_type=jnp.float32)  6.12 us
    broadcast_in_dim x1, other arithmetic, body(): grad_output[None]  4.9 us
    dot_general x1, matrix products, body(): combined = jnp.dot(hidden, tap_center, preferred_element_type=jnp.float32)  4.44 us
  transfers between devices with their start and end apart: 4, of which 2 were waited for; matrix products, arithmetic and copies ran while one was open for 5% of the time, Pallas kernels for 0%

commit v1 on v0

--- a/solution.py
+++ b/solution.py
@@ -78,7 +78,7 @@
     grad_hidden = grad_hidden + before_valid * terms_before + after_valid * terms_after
     grad_signal, input_terms = input_vjp(grad_hidden)
     grad_output = (upstream.astype(jnp.float32) + grad_signal).astype(jnp.bfloat16)
-    summed = lax.psum((input_terms, middle_terms), ("seq", "batch"))
+    summed = lax.psum(lax.psum((input_terms, middle_terms), "batch"), "seq")
     factor = 1.0 / math.sqrt(lax.axis_size("batch") * seq_count * shard_rows)
     return (output[None], grad_output[None], summed[0] * factor, summed[1] * factor)
 

time: 217 us -> 242 us (1.12)
  blocking collectives: 41.6 us -> 66.4 us
    psum x1 -> x2, blocking collectives: 41.6 us -> 66.4 us  [body(): summed = lax.psum(lax.psum((input_terms, middle_terms), 'batch'), 'seq')]
where the time goes in v1:
time: 242 us; the launch traced here: 241 us
  waiting for transfers between devices  123 us (51%)
  blocking collectives  66.4 us (27%)
  matrix products  26.1 us (11%)
  starting transfers between devices  13.2 us (5%)
  other arithmetic  11.9 us (5%)
    ppermute x4, waiting for transfers between devices, shifted(): return lax.ppermute(x, axis, pairs)  123 us
    psum x2, blocking collectives, body(): summed = lax.psum(lax.psum((input_terms, middle_terms), 'batch'), 'seq')  66.4 us
    ppermute x4, starting transfers between devices, shifted(): return lax.ppermute(x, axis, pairs)  13.2 us
    dot_general x1, matrix products, body(): jnp.dot(grad_combined, tap_center.T, preferred_element_type=jnp.float32)  6.12 us
    broadcast_in_dim x1, other arithmetic, body(): grad_output[None]  4.9 us
  transfers between devices with their start and end apart: 4, of which 2 were waited for; matrix products, arithmetic and copies ran while one was open for 5% of the time, Pallas kernels for 0%

profile of v1, /device:TPU:0, one launch (start us, length us, event | category | flops | bytes accessed | tf_op | source)
XLA Modules:
  0.0 241.3 jit_solution(3740659526648683788)
XLA Ops:
  0.6 0.0 copy-start
  0.6 0.0 copy-start.1
  0.7 0.0 copy-start.4
  0.7 0.0 copy-start.6
  0.7 1.9 fusion.16
  2.6 0.1 copy-done.1
  2.7 3.2 %fusion.12 = bf16[512,1536]{1,0:T(8,128)(2,1)} fusion(bf16[1,512,1536]{2,1,0:T(8,128)(2,1)S(1)} %copy-done.1, f32[1536]{0:T(1024)} %param.10, f32[512]{0:T(512)S(1)} %fusion.88), kind=kLoop, calls=%fused_computation.18 | loop fusion | flops 9437184 | bytes 3153920 | tf_op jit(solution)/shard_map/convert_element_type | solution.py:50
  5.9 6.0 %collective-permute-start = (bf16[512,1536]{1,0:T(8,128)(2,1)}, bf16[512,1536]{1,0:T(8,128)(2,1)}, u32[]{:S(2)}, u32[]{:S(2)}) collective-permute-start(bf16[512,1536]{1,0:T(8,128)(2,1)} %fusion.12), channel_id=1, source_target_pairs={{0,4},{2,6},{4,8},{6,10},{8,12},{10,14},{12,16},{14,18},{16,20},{1... | collective-permute-start | bytes 4718600 | tf_op jit(solution)/shard_map/ppermute | solution.py:14
  11.9 1.3 collective-permute-start.1
  13.2 0.0 copy-done.6
  13.2 0.2 reduce-window.8
  13.4 0.1 convert_reduce_fusion.2
  13.5 0.0 copy-done.4
  13.5 4.4 %fusion.42 = f32[512,768]{1,0:T(8,128)S(1)} fusion(bf16[3,1536,768]{2,1,0:T(8,128)(2,1)} %param.11, bf16[1,512,1536]{2,1,0:T(8,128)(2,1)} %param.7, f32[1536]{0:T(1024)S(1)} %copy-done.4, f32[512]{0:T(512)S(1)} %fusion.88), kind=kOutput, calls=%fused_computation.51 | convolution fusion | flops 1217396736 | bytes 5513216 | tf_op jit(solution)/shard_map/dot_general | solution.py:53
  17.9 60.5 %collective-permute-done = bf16[512,1536]{1,0:T(8,128)(2,1)} collective-permute-done((bf16[512,1536]{1,0:T(8,128)(2,1)}, bf16[512,1536]{1,0:T(8,128)(2,1)}, u32[]{:S(2)}, u32[]{:S(2)}) %collective-permute-start) | collective-permute-done | bytes 1572896 | tf_op jit(solution)/shard_map/ppermute | solution.py:14
  78.4 3.5 %fusion.38 = f32[512,768]{1,0:T(8,128)S(1)} fusion(bf16[512,1536]{1,0:T(8,128)(2,1)} %collective-permute-done, bf16[3,1536,768]{2,1,0:T(8,128)(2,1)} %param.11), kind=kOutput, calls=%fused_computation.47 | convolution fusion | flops 1207959552 | bytes 5505024 | tf_op jit(solution)/shard_map/dot_general | solution.py:54
  81.9 0.0 collective-permute-done.1
  81.9 0.0 copy-start.3
  82.0 0.0 copy-start.5
  82.0 3.8 %multiply_reduce_fusion.2 = (f32[512]{0:T(512)S(1)}, f32[512,768]{1,0:T(8,128)S(1)}) fusion(bf16[512,1536]{1,0:T(8,128)(2,1)} %collective-permute-done.1, bf16[3,1536,768]{2,1,0:T(8,128)(2,1)} %param.11, f32[512]{0:T(512)S(1)} %get-tuple-element.16, f32[512,768]{1,0:T(8,128)S(1)} %fusion.42, f32[512,768]{1,0:T(8,128)S(1)} %fusion.38, ...), kind=kOutput, calls=%fused_computation.75 | convolution fusion | flops 1210318336 | bytes 8656896 | tf_op jit(solution)/shard_map/dot_general | solution.py:57
  85.8 0.0 slice-start
  85.8 0.0 copy-done
  85.8 0.0 copy-done.3
  85.8 0.0 copy-done.5
  85.9 0.0 slice-start.1
  85.9 2.5 %multiply_reduce_fusion = (f32[768]{0:T(1024)S(1)}, f32[512]{0:T(512)S(1)}, f32[512,768]{1,0:T(8,128)S(1)}) fusion(f32[512,768]{1,0:T(8,128)S(1)} %get-tuple-element.18, f32[512]{0:T(512)S(1)} %fusion.89, f32[768]{0:T(1024)S(1)} %copy-done.5, bf16[768,1536]{1,0:T(8,128)(2,1)S(1)} %copy-done, bf16[1,512,1536]{2,1,0:T(8,128)(2,1)S(1)} %copy-done.3), kind=kOutput, calls=%fused_computation.72 | convolution fusion | flops 1218181888 | bytes 7088128 | tf_op jit(solution)/shard_map/dot_general | solution.py:66
  88.4 0.4 fusion.58
  88.8 0.0 slice-done
  88.8 0.1 slice-done.1
  88.9 1.4 convolution_convert_fusion
  90.3 0.0 copy-start.2
  90.4 1.4 convolution_convert_fusion.1
  91.8 4.5 %collective-permute-start.2 = (bf16[512,1536]{1,0:T(8,128)(2,1)S(1)}, bf16[512,1536]{1,0:T(8,128)(2,1)S(1)}, u32[]{:S(2)}, u32[]{:S(2)}) collective-permute-start(bf16[512,1536]{1,0:T(8,128)(2,1)S(1)} %convolution_convert_fusion.1), channel_id=1, source_target_pairs={{0,4},{2,6},{4,8},{6,10},{8,12},{10,14},{12,16},{14,18},{16,20},{1... | collective-permute-start | bytes 4718600 | tf_op jit(solution)/shard_map/ppermute | solution.py:14
  96.3 1.5 collective-permute-start.3
  97.8 0.0 copy-done.2
  97.8 2.8 %fusion.33 = bf16[1,512,1536]{2,1,0:T(8,128)(2,1)} fusion(bf16[768,1536]{1,0:T(8,128)(2,1)S(1)} %copy-done, bf16[1,512,1536]{2,1,0:T(8,128)(2,1)S(1)} %copy-done.2, f32[512,768]{1,0:T(8,128)S(1)} %get-tuple-element.18, f32[768]{0:T(1024)S(1)} %copy-done.5, f32[512]{0:T(512)S(1)} %fusion.89), kind=kOutput, calls=%fused_computation.41 | convolution fusion | flops 1214644224 | bytes 7083008 | tf_op jit(solution)/shard_map/dot_general | solution.py:64
  100.6 62.0 %collective-permute-done.2 = bf16[512,1536]{1,0:T(8,128)(2,1)S(1)} collective-permute-done((bf16[512,1536]{1,0:T(8,128)(2,1)S(1)}, bf16[512,1536]{1,0:T(8,128)(2,1)S(1)}, u32[]{:S(2)}, u32[]{:S(2)}) %collective-permute-start.2) | collective-permute-done | bytes 1572896 | tf_op jit(solution)/shard_map/ppermute | solution.py:14
  162.6 0.0 collective-permute-done.3
  162.7 6.1 %fusion.15 = (f32[1536]{0:T(1024)S(1)}, f32[512]{0:T(512)S(1)}, f32[512,1536]{1,0:T(8,128)}) fusion(bf16[1,512,1536]{2,1,0:T(8,128)(2,1)S(1)} %copy-done.2, f32[512]{0:T(512)S(1)} %fusion.88, f32[1536]{0:T(1024)S(1)} %copy-done.4, bf16[512,1536]{1,0:T(8,128)(2,1)S(1)} %collective-permute-done.3, f32[512]{0:T(512)S(1)} %get-tuple-element.16, ...), kind=kOutput, calls=%fused_computation.21 | convolution fusion | flops 1233909760 | bytes 11032576 | tf_op jit(solution)/shard_map/dot_general | solution.py:69
  168.8 8.1 %all-reduce.1 = (f32[1536]{0:T(1024)S(1)}, f32[768]{0:T(1024)S(1)}) all-reduce(f32[1536]{0:T(1024)S(1)} %get-tuple-element.4, f32[768]{0:T(1024)S(1)} %get-tuple-element.6), channel_id=1, replica_groups=mesh['seq'=16,'batch'=2] {'batch'}, use_global_device_ids=true, to_apply=%region_9.10 | all-reduce | flops 2304 | bytes 18432 | tf_op jit(solution)/shard_map/psum | solution.py:81
  176.9 58.3 %all-reduce = (f32[1536]{0:T(1024)S(1)}, f32[768]{0:T(1024)S(1)}) all-reduce(f32[1536]{0:T(1024)S(1)} %get-tuple-element.13, f32[768]{0:T(1024)S(1)} %get-tuple-element.14), channel_id=1, replica_groups=mesh['seq'=16,'batch'=2] {'seq'}, use_global_device_ids=true, to_apply=%region_10.11 | all-reduce | flops 2304 | bytes 18432 | tf_op jit(solution)/shard_map/psum | solution.py:81
  235.2 0.6 broadcast_multiply_fusion
  235.8 0.6 broadcast_multiply_fusion.1
  236.4 4.9 %fusion.59 = bf16[1,512,1536]{2,1,0:T(8,128)(2,1)} fusion(bf16[1,512,1536]{2,1,0:T(8,128)(2,1)} %param.7, f32[512,1536]{1,0:T(8,128)} %get-tuple-element.20, bf16[1,512,1536]{2,1,0:T(8,128)(2,1)} %param.8, f32[512]{0:T(512)S(1)} %multiply_multiply_fusion.6, f32[1536]{0:T(1024)S(1)} %copy-done.4, f32[512]{0:T(512)S(1)} %fusion.88), kind=kLoop, calls=%fused_computation.68 | loop fusion | flops 7077888 | bytes 7874560 | tf_op jit(solution)/shard_map/broadcast_in_dim | solution.py:83
  (8 shorter events, 0.1 us)
Async XLA Ops:
  0.6 85.2 %copy-start = (bf16[768,1536]{1,0:T(8,128)(2,1)S(1)}, bf16[768,1536]{1,0:T(8,128)(2,1)}, u32[]{:S(2)}) copy-start(bf16[768,1536]{1,0:T(8,128)(2,1)} %param.13) | copy-start | bytes 7077892
  0.6 2.0 copy-start.1
  0.7 12.8 %copy-start.4 = (f32[1536]{0:T(1024)S(1)}, f32[1536]{0:T(1024)}, u32[]{:S(2)}) copy-start(f32[1536]{0:T(1024)} %param.10) | copy-start | bytes 18436
  0.7 12.5 %copy-start.6 = (s32[1,4]{1,0:T(1,128)S(1)}, s32[1,4]{1,0:T(1,128)}, u32[]{:S(2)}) copy-start(s32[1,4]{1,0:T(1,128)} %param.9) | copy-start | bytes 52
  5.9 72.5 %collective-permute-start = (bf16[512,1536]{1,0:T(8,128)(2,1)}, bf16[512,1536]{1,0:T(8,128)(2,1)}, u32[]{:S(2)}, u32[]{:S(2)}) collective-permute-start(bf16[512,1536]{1,0:T(8,128)(2,1)} %fusion.12), channel_id=1, source_target_pairs={{0,4},{2,6},{4,8},{6,10},{8,12},{10,14},{12,16},{14,18},{16,20},{1... | collective-permute-start | bytes 4718600 | tf_op jit(solution)/shard_map/ppermute | solution.py:14
  11.9 70.0 %collective-permute-start.1 = (bf16[512,1536]{1,0:T(8,128)(2,1)}, bf16[512,1536]{1,0:T(8,128)(2,1)}, u32[]{:S(2)}, u32[]{:S(2)}) collective-permute-start(bf16[512,1536]{1,0:T(8,128)(2,1)} %fusion.12), channel_id=1, source_target_pairs={{4,0},{6,2},{8,4},{10,6},{12,8},{14,10},{16,12},{18,14},{20,16},{2... | collective-permute-start | bytes 4718600 | tf_op jit(solution)/shard_map/ppermute | solution.py:14
  81.9 3.9 %copy-start.3 = (bf16[1,512,1536]{2,1,0:T(8,128)(2,1)S(1)}, bf16[1,512,1536]{2,1,0:T(8,128)(2,1)}, u32[]{:S(2)}) copy-start(bf16[1,512,1536]{2,1,0:T(8,128)(2,1)} %param.8) | copy-start | bytes 4718596
  82.0 3.9 %copy-start.5 = (f32[768]{0:T(1024)S(1)}, f32[768]{0:T(1024)}, u32[]{:S(2)}) copy-start(f32[768]{0:T(1024)} %param.12) | copy-start | bytes 9220
  85.8 3.0 %slice-start = ((s8[7077888]{0:T(1024)(128)(4,1)}), s8[4194304]{0:T(1024)(128)(4,1)S(1)}, s32[]{:S(2)}) async-start(s8[7077888]{0:T(1024)(128)(4,1)} %bitcast.116), calls=%async_computation | async-start | bytes 8388608
  85.9 3.1 %slice-start.1 = ((s8[7077888]{0:T(1024)(128)(4,1)}), s8[2883584]{0:T(1024)(128)(4,1)S(1)}, s32[]{:S(2)}) async-start(s8[7077888]{0:T(1024)(128)(4,1)} %bitcast.116), calls=%async_computation.1 | async-start | bytes 5767168
  90.3 7.4 %copy-start.2 = (bf16[1,512,1536]{2,1,0:T(8,128)(2,1)S(1)}, bf16[1,512,1536]{2,1,0:T(8,128)(2,1)}, u32[]{:S(2)}) copy-start(bf16[1,512,1536]{2,1,0:T(8,128)(2,1)} %param.7) | copy-start | bytes 4718596
  91.8 70.9 %collective-permute-start.2 = (bf16[512,1536]{1,0:T(8,128)(2,1)S(1)}, bf16[512,1536]{1,0:T(8,128)(2,1)S(1)}, u32[]{:S(2)}, u32[]{:S(2)}) collective-permute-start(bf16[512,1536]{1,0:T(8,128)(2,1)S(1)} %convolution_convert_fusion.1), channel_id=1, source_target_pairs={{0,4},{2,6},{4,8},{6,10},{8,12},{10,14},{12,16},{14,18},{16,20},{1... | collective-permute-start | bytes 4718600 | tf_op jit(solution)/shard_map/ppermute | solution.py:14
  96.3 66.4 %collective-permute-start.3 = (bf16[512,1536]{1,0:T(8,128)(2,1)S(1)}, bf16[512,1536]{1,0:T(8,128)(2,1)S(1)}, u32[]{:S(2)}, u32[]{:S(2)}) collective-permute-start(bf16[512,1536]{1,0:T(8,128)(2,1)S(1)} %convolution_convert_fusion), channel_id=1, source_target_pairs={{4,0},{6,2},{8,4},{10,6},{12,8},{14,10},{16,12},{18,14},{20,16},{2... | collective-permute-start | bytes 4718600 | tf_op jit(solution)/shard_map/ppermute | solution.py:14
